TPU v7x, 256 devices: a whole 4x4x8 slice. The times are simulated.
256 devices in a mesh: tm: 32 (over x_lo, z, core), cell: 8 (over y, x_hi).
Axes of the slice: x: 4 (x_hi: 2, x_lo: 2; x = x_hi * 2 + x_lo), y: 4, z: 8, core: 2. Of those that a mesh axis runs over, the one named last changes fastest.
Arguments:
- velocity: bfloat16 [4096, 512, 96], P('cell', 'tm'), may hold values from -6 to 6
- cell_coords: int32 [4096, 3], P('cell'), may hold values from 0 to 15, as said below
- q_coords: int32 [512, 3], replicated, may hold values from 0 to 15
- eigvecs: float32 [512, 2, 96, 96], P(('tm', 'cell')), may hold values from -0.4375 to 0.4375
Outputs:
- power: float32 [512, 96, 512], P(('tm', 'cell'))
Inputs may be any that keep to these rules, and one draw needn't show every extreme that they name: `cell_coords`: every row names a distinct lattice position, each coordinate in 0 to 15.
All inputs are finite; a program needn't handle non-finite values.
Results may differ from a plain program's by a relative error of at most 0.015.
Values may be sent and summed in bfloat16 or wider, within the bound.
No kernel may reach another device: no remote copies, remote signals or barrier semaphores. Data moves between devices by JAX's collectives and lax.ppermute only.
A program may use at most 64 MiB of HBM per device.

v0:
```python
import math
import jax
import jax.numpy as jnp
from jax import lax
from jax.sharding import PartitionSpec as P

L = 16


def phase_rows(q_coords, cell_coords):
    products = (
        q_coords[:, None, 0] * cell_coords[None, :, 0]
        + q_coords[:, None, 1] * cell_coords[None, :, 1]
        + q_coords[:, None, 2] * cell_coords[None, :, 2]
    )
    step = jnp.arange(4, dtype=jnp.float32) * (2.0 * math.pi / L)
    cos_table = jnp.cos(step).astype(jnp.bfloat16)
    sin_table = (-jnp.sin(step)).astype(jnp.bfloat16)
    bit0 = products & 1 != 0
    bit1 = products & 2 != 0
    bit2 = products & 4 != 0
    bit3 = products & 8 != 0
    real = jnp.where(
        bit1,
        jnp.where(bit0, cos_table[3], cos_table[2]),
        jnp.where(bit0, cos_table[1], cos_table[0]),
    )
    imag = jnp.where(
        bit1,
        jnp.where(bit0, sin_table[3], sin_table[2]),
        jnp.where(bit0, sin_table[1], sin_table[0]),
    )
    real, imag = (jnp.where(bit2, imag, real), jnp.where(bit2, -real, imag))
    real, imag = (jnp.where(bit3, -real, real), jnp.where(bit3, -imag, imag))
    return jnp.stack([real, imag], axis=1)


def twiddles(frames):
    inner = 16
    outer = frames // inner
    w = jnp.arange(frames, dtype=jnp.int32)
    a = jnp.arange(outer, dtype=jnp.int32)
    b = jnp.arange(inner, dtype=jnp.int32)
    coarse = (a[:, None] * w[None, :] % outer).astype(jnp.float32) * (2.0 * math.pi / outer)
    fine = (b[:, None] * w[None, :] % frames).astype(jnp.float32) * (2.0 * math.pi / frames)
    cos_c, sin_c = (jnp.cos(coarse)[:, None, :], jnp.sin(coarse)[:, None, :])
    cos_f, sin_f = (jnp.cos(fine)[None, :, :], jnp.sin(fine)[None, :, :])
    cosines = (cos_c * cos_f - sin_c * sin_f).reshape(frames, frames)
    sines = (sin_c * cos_f + cos_c * sin_f).reshape(frames, frames)
    return (cosines, sines)


def local(velocity, cell_coords, q_coords, eigvecs):
    n_tm = lax.axis_size("tm")
    n_cell = lax.axis_size("cell")
    n_dev = n_tm * n_cell
    cell_dev, frames_dev, branches = velocity.shape
    q_total = q_coords.shape[0]
    q_local = q_total // n_dev
    frames = frames_dev * n_tm
    frames_each = frames_dev // n_cell
    spread = velocity.reshape(cell_dev, n_cell, frames_each * branches)
    all_cells = lax.all_to_all(spread, "cell", split_axis=1, concat_axis=0, tiled=True)
    all_cells = all_cells.reshape(cell_dev * n_cell, frames_each * branches)
    all_coords = lax.all_gather(cell_coords, "cell", axis=0, tiled=True)
    table = phase_rows(q_coords, all_coords).reshape(2 * q_total, cell_dev * n_cell)
    modes = jnp.dot(table, all_cells, preferred_element_type=jnp.float32)
    modes = modes.astype(jnp.bfloat16).reshape(n_dev, q_local, 2, frames_each, branches)
    collected = lax.all_to_all(modes, ("tm", "cell"), split_axis=0, concat_axis=0, tiled=True)
    scale = 1.0 / math.sqrt(cell_dev * n_cell)
    e_real = eigvecs[:, 0] * scale
    e_imag = eigvecs[:, 1] * scale
    e_block = jnp.stack(
        [jnp.concatenate([e_real, -e_imag], axis=2), jnp.concatenate([e_imag, e_real], axis=2)],
        axis=1,
    )
    highest = lax.Precision.HIGHEST
    amplitude = jnp.einsum(
        "sjrfk,jrkc->jsfc", collected.astype(jnp.float32), e_block, precision=highest
    ).reshape(q_local, frames, 2 * branches)
    cosines, sines = twiddles(frames)
    basis = jnp.concatenate([cosines, sines], axis=1)
    projected = jnp.einsum("jts,tw->jsw", amplitude, basis, precision=highest)
    on_cos = projected[:, :, :frames]
    on_sin = projected[:, :, frames:]
    out_real = on_cos[:, :branches] + on_sin[:, branches:]
    out_imag = on_cos[:, branches:] - on_sin[:, :branches]
    return (out_real * out_real + out_imag * out_imag) / frames


def solution(mesh):
    in_specs = (P("cell", "tm", None), P("cell", None), P(), P(("tm", "cell"), None, None, None))
    out_specs = P(("tm", "cell"), None, None)
    return jax.shard_map(local, mesh=mesh, in_specs=in_specs, out_specs=out_specs, check_vma=False)
```

profile of v0, /device:TPU:1, one launch (start us, length us, event | category | flops | bytes accessed | tf_op | source)
XLA Modules:
  0.0 152.7 jit_solution(2938117541314478069)
XLA Ops:
  0.0 7.5 %all-to-all-start = ((bf16[512,8,192]{0,2,1:T(8,128)(2,1)}), bf16[512,8,192]{0,2,1:T(8,128)(2,1)S(1)}, u32[]{:S(2)}, u32[]{:S(2)}) async-start(bf16[512,8,192]{0,2,1:T(8,128)(2,1)} %bitcast.57), calls=%async_computation | async-start | bytes 3145728 | tf_op jit(solution)/shard_map/all_to_all | solution.py:63
  7.6 0.6 fusion.34
  8.2 0.7 fusion.33
  8.9 42.0 %all_gather.3 = s32[4096,3]{0,1:T(4,128)S(1)} all-gather(s32[512,3]{0,1:T(4,128)} %param.5), channel_id=1, replica_groups=mesh['tm'=32,'cell'=8] {'cell'}, dimensions={0}, use_global_device_ids=true | all-gather | bytes 55296 | tf_op jit(solution)/shard_map/all_gather | solution.py:65
  50.9 0.8 fusion.32
  51.7 13.9 %negate_select_fusion.1 = (bf16[512,1,4096]{2,0,1:T(8,128)(2,1)S(1)}, bf16[512,1,4096]{2,0,1:T(8,128)(2,1)}) fusion(bf16[]{:T(256)} %bitcast.13, bf16[]{:T(256)} %bitcast.12, bf16[]{:T(256)} %bitcast.11, bf16[]{:T(256)} %bitcast.10, bf16[]{:T(256)} %bitcast.9, bf16[]{:T(256)} %bitcast.8, bf16[]{:T(256)} %bitcast.7, bf16[]{:T(256)} %bitcast.6, ...), kind=kLoop, calls=%fused_computation.7 | loop fusion | flops 67108864 | bytes 8443920 | tf_op jit(solution)/shard_map/jit(_where)/select_n | solution.py:34
  65.6 6.2 %pad_maximum_fusion = bf16[512,2,4096]{2,0,1:T(8,128)(2,1)} fusion(bf16[512,1,4096]{2,0,1:T(8,128)(2,1)} %get-tuple-element.15, bf16[512,1,4096]{2,0,1:T(8,128)(2,1)S(1)} %get-tuple-element.14), kind=kLoop, calls=%fused_computation | loop fusion | flops 4194304 | bytes 16777216 | tf_op jit(solution)/shard_map/stack | solution.py:35
  71.7 16.4 %copy.35 = bf16[512,2,4096]{2,1,0:T(2,128)(2,1)} copy(bf16[512,2,4096]{2,0,1:T(8,128)(2,1)} %pad_maximum_fusion) | data formatting | bytes 16777216 | tf_op jit(solution)/shard_map/stack | solution.py:35
  88.1 0.0 copy-start
  88.1 13.2 %reshape.499 = bf16[1024,4096]{1,0:T(8,128)(2,1)} reshape(bf16[512,2,4096]{2,1,0:T(2,128)(2,1)} %copy.35) | data formatting | bytes 16777216 | tf_op jit(solution)/shard_map/reshape | solution.py:66
  101.3 0.0 copy-done
  101.3 0.1 copy.48
  101.4 0.0 all-to-all-done
  101.5 0.2 copy.49
  101.6 6.3 %convolution_convert_fusion = bf16[1024,192]{0,1:T(8,128)(2,1)S(1)} fusion(bf16[1024,4096]{1,0:T(8,128)(2,1)} %reshape.499, bf16[4096,192]{0,1:T(8,128)(2,1)S(1)} %bitcast.58), kind=kOutput, calls=%fused_computation.15 | convolution fusion | flops 1610809344 | bytes 10354688 | tf_op jit(solution)/shard_map/dot_general | solution.py:67
  108.0 0.2 copy.37
  108.2 0.3 reshape.502
  108.5 1.2 copy.38
  109.6 16.1 %all-to-all-start.1 = ((bf16[256,2,2,2,96]{4,2,3,1,0:T(2,128)(2,1)}), bf16[256,2,2,2,96]{4,2,3,1,0:T(2,128)(2,1)S(1)}, u32[]{:S(2)}, u32[]{:S(2)}) async-start(bf16[256,2,2,2,96]{4,2,3,1,0:T(2,128)(2,1)} %copy.38), calls=%async_computation.1 | async-start | bytes 1048576 | tf_op jit(solution)/shard_map/all_to_all | solution.py:69
  125.8 0.1 fusion.25
  125.9 0.1 copy.47
  126.0 0.3 fusion.22
  126.4 0.3 multiply_subtract_fusion
  126.7 19.2 %all-to-all-done.1 = bf16[256,2,2,2,96]{4,2,3,1,0:T(2,128)(2,1)S(1)} async-done(((bf16[256,2,2,2,96]{4,2,3,1,0:T(2,128)(2,1)}), bf16[256,2,2,2,96]{4,2,3,1,0:T(2,128)(2,1)S(1)}, u32[]{:S(2)}, u32[]{:S(2)}) %all-to-all-start.1) | async-done | bytes 393248 | tf_op jit(solution)/shard_map/all_to_all | solution.py:69
  145.9 1.6 %convolution_bitcast_fusion = f32[2,256,2,192]{1,3,2,0:T(8,128)} fusion(bf16[256,2,2,2,96]{4,2,3,1,0:T(2,128)(2,1)S(1)} %all-to-all-done.1, f32[2,1,96,192]{2,3,1,0:T(8,128)S(1)} %get-tuple-element.10, f32[2,1,96,192]{2,3,1,0:T(8,128)S(1)} %get-tuple-element.9), kind=kOutput, calls=%fused_computation.14 | convolution fusion | flops 453058560 | bytes 1474560 | tf_op jit(solution)/shard_map/sjrfk,jrkc->jsfc/dot_general | solution.py:78
  147.5 1.5 %copy.43 = f32[2,256,2,192]{3,0,2,1:T(2,128)S(1)} copy(f32[2,256,2,192]{1,3,2,0:T(8,128)} %convolution_bitcast_fusion) | data formatting | bytes 1572864 | tf_op jit(solution)/shard_map/sjrfk,jrkc->jsfc/dot_general | solution.py:78
  149.0 2.7 %fusion = f32[2,192,1024]{2,1,0:T(8,128)S(1)} fusion(f32[512,512]{1,0:T(8,128)S(1)} %bitcast.56, f32[512,512]{1,0:T(8,128)S(1)} %bitcast.55, f32[2,512,192]{2,0,1:T(2,128)S(1)} %bitcast.54), kind=kOutput, calls=%fused_computation.11 | convolution fusion | flops 2416443392 | bytes 4456448 | tf_op jit(solution)/shard_map/jts,tw->jsw/dot_general | solution.py:83
  151.8 0.9 fusion.7
  (7 shorter events, 0.2 us)
Async XLA Ops:
  0.0 101.4 %all-to-all-start = ((bf16[512,8,192]{0,2,1:T(8,128)(2,1)}), bf16[512,8,192]{0,2,1:T(8,128)(2,1)S(1)}, u32[]{:S(2)}, u32[]{:S(2)}) async-start(bf16[512,8,192]{0,2,1:T(8,128)(2,1)} %bitcast.57), calls=%async_computation | async-start | bytes 3145728 | tf_op jit(solution)/shard_map/all_to_all | solution.py:63
  88.1 13.2 %copy-start = (f32[2,2,96,96]{3,2,1,0:T(8,128)S(1)}, f32[2,2,96,96]{3,2,1,0:T(8,128)}, u32[]{:S(2)}) copy-start(f32[2,2,96,96]{3,2,1,0:T(8,128)} %param.7) | copy-start | bytes 442372
  109.6 36.3 %all-to-all-start.1 = ((bf16[256,2,2,2,96]{4,2,3,1,0:T(2,128)(2,1)}), bf16[256,2,2,2,96]{4,2,3,1,0:T(2,128)(2,1)S(1)}, u32[]{:S(2)}, u32[]{:S(2)}) async-start(bf16[256,2,2,2,96]{4,2,3,1,0:T(2,128)(2,1)} %copy.38), calls=%async_computation.1 | async-start | bytes 1048576 | tf_op jit(solution)/shard_map/all_to_all | solution.py:69
where the time goes:
time: 153 us
  blocking collectives  42 us (27%)
  local copies, waits for them, and re-layouts  35.2 us (23%)
  starting transfers between devices  23.6 us (15%)
  other arithmetic  21.8 us (14%)
  waiting for transfers between devices  19.2 us (13%)
  matrix products  10.7 us (7%)
    all_gather x1, blocking collectives, local(): all_coords = lax.all_gather(cell_coords, 'cell', axis=0, tiled=True)  42 us
    all_to_all x1, waiting for transfers between devices, local(): lax.all_to_all(modes, ('tm', 'cell'), split_axis=0, concat_axis=0, tiled=...  19.2 us
    another operation x1, local copies, waits for them, and re-layouts, phase_rows(): return jnp.stack([real, imag], axis=1)  16.4 us
    all_to_all x1, starting transfers between devices, local(): lax.all_to_all(modes, ('tm', 'cell'), split_axis=0, concat_axis=0, tiled=...  16.1 us
    select_n x1, other arithmetic, phase_rows(): real, imag = (jnp.where(bit3, -real, real), jnp.where(bit3, -imag, imag))  13.9 us
    reshape x1, local copies, waits for them, and re-layouts, local(): phase_rows(q_coords, all_coords).reshape(2 * q_total, cell_dev * n_cell)  13.2 us
    all_to_all x1, starting transfers between devices, local(): lax.all_to_all(spread, 'cell', split_axis=1, concat_axis=0, tiled=True)  7.48 us
    dot_general x1, matrix products, local(): modes = jnp.dot(table, all_cells, preferred_element_type=jnp.float32)  6.34 us
  transfers between devices with their start and end apart: 2, of which 1 were waited for; matrix products, arithmetic and copies ran while one was open for 35% of the time, Pallas kernels for 0%

commit v1 on v0

--- a/solution.py
+++ b/solution.py
@@ -5,6 +5,13 @@
 from jax.sharding import PartitionSpec as P
 
 L = 16
+
+
+def swapped_in(x, name, dim):
+    size = lax.axis_size(name)
+    pieces = jnp.stack([x for _ in range(size)])
+    pieces = lax.all_to_all(pieces, name, split_axis=0, concat_axis=0)
+    return jnp.concatenate(pieces, axis=dim)
 
 
 def phase_rows(q_coords, cell_coords):
@@ -62,7 +69,7 @@
     spread = velocity.reshape(cell_dev, n_cell, frames_each * branches)
     all_cells = lax.all_to_all(spread, "cell", split_axis=1, concat_axis=0, tiled=True)
     all_cells = all_cells.reshape(cell_dev * n_cell, frames_each * branches)
-    all_coords = lax.all_gather(cell_coords, "cell", axis=0, tiled=True)
+    all_coords = swapped_in(cell_coords, "cell", 0)
     table = phase_rows(q_coords, all_coords).reshape(2 * q_total, cell_dev * n_cell)
     modes = jnp.dot(table, all_cells, preferred_element_type=jnp.float32)
     modes = modes.astype(jnp.bfloat16).reshape(n_dev, q_local, 2, frames_each, branches)

time: 153 us -> 121 us (0.79)
  blocking collectives: 42 us -> 0 us
  starting transfers between devices: 23.6 us -> 27.5 us
  waiting for transfers between devices: 19.2 us -> 22.6 us
  local copies, waits for them, and re-layouts: 35.2 us -> 37.5 us
    all_gather x1 -> x0, blocking collectives: 42 us -> none  [local(): all_coords = lax.all_gather(cell_coords, 'cell', axis=0, tiled=True)]
    all_to_all x0 -> x1, starting transfers between devices: none -> 7.48 us  [swapped_in(): pieces = lax.all_to_all(pieces, name, split_axis=0, concat_axis=0)]
    all_to_all x1, starting transfers between devices: 7.48 us -> 3.58 us  [local(): lax.all_to_all(spread, 'cell', split_axis=1, concat_axis=0, tiled=True)]
    all_to_all x0 -> x1, waiting for transfers between devices: none -> 3.39 us  [swapped_in(): pieces = lax.all_to_all(pieces, name, split_axis=0, concat_axis=0)]
  transfers between devices with their start and end apart: 2 -> 3, of which waited for: 1 -> 2; matrix products, arithmetic and copies ran while one was open for 35% -> 45% of each run, Pallas kernels for 0% -> 0%
where the time goes in v1:
time: 121 us; the launch traced here: 120 us
  local copies, waits for them, and re-layouts  37.5 us (31%)
  starting transfers between devices  27.5 us (23%)
  waiting for transfers between devices  22.6 us (19%)
  other arithmetic  21.8 us (18%)
  matrix products  10.7 us (9%)
    all_to_all x1, waiting for transfers between devices, local(): lax.all_to_all(modes, ('tm', 'cell'), split_axis=0, concat_axis=0, tiled=...  19.2 us
    all_to_all x1, starting transfers between devices, local(): lax.all_to_all(modes, ('tm', 'cell'), split_axis=0, concat_axis=0, tiled=...  16.5 us
    another operation x1, local copies, waits for them, and re-layouts, phase_rows(): return jnp.stack([real, imag], axis=1)  16.4 us
    select_n x1, other arithmetic, phase_rows(): real, imag = (jnp.where(bit3, -real, real), jnp.where(bit3, -imag, imag))  13.9 us
    reshape x1, local copies, waits for them, and re-layouts, local(): phase_rows(q_coords, all_coords).reshape(2 * q_total, cell_dev * n_cell)  13.1 us
    all_to_all x1, starting transfers between devices, swapped_in(): pieces = lax.all_to_all(pieces, name, split_axis=0, concat_axis=0)  7.48 us
    dot_general x1, matrix products, local(): modes = jnp.dot(table, all_cells, preferred_element_type=jnp.float32)  6.33 us
    another operation x1, other arithmetic, phase_rows(): return jnp.stack([real, imag], axis=1)  6.18 us
  transfers between devices with their start and end apart: 3, of which 2 were waited for; matrix products, arithmetic and copies ran while one was open for 45% of the time, Pallas kernels for 0%

profile of v1, /device:TPU:1, one launch (start us, length us, event | category | flops | bytes accessed | tf_op | source)
XLA Modules:
  0.0 120.3 jit_solution(16276872743622371757)
XLA Ops:
  0.0 1.3 %stack.10 = s32[8,512,3]{1,2,0:T(4,128)} broadcast(s32[512,3]{0,1:T(4,128)} %param.5), dimensions={1,2} | broadcast | bytes 55296 | tf_op jit(solution)/shard_map/stack | solution.py:12
  1.3 7.5 %all-to-all-start = ((s32[8,512,3]{1,2,0:T(4,128)}), s32[8,512,3]{1,2,0:T(4,128)S(1)}, u32[]{:S(2)}, u32[]{:S(2)}) async-start(s32[8,512,3]{1,2,0:T(4,128)} %stack.10), calls=%async_computation | async-start | bytes 131072 | tf_op jit(solution)/shard_map/all_to_all | solution.py:13
  8.9 0.7 fusion.33
  9.6 0.8 fusion.32
  10.4 1.0 fusion.30
  11.3 0.1 copy.49
  11.5 0.7 fusion.34
  12.1 3.4 %all-to-all-done = s32[8,512,3]{1,2,0:T(4,128)S(1)} async-done(((s32[8,512,3]{1,2,0:T(4,128)}), s32[8,512,3]{1,2,0:T(4,128)S(1)}, u32[]{:S(2)}, u32[]{:S(2)}) %all-to-all-start) | async-done | bytes 49184 | tf_op jit(solution)/shard_map/all_to_all | solution.py:13
  15.5 3.6 %all-to-all-start.1 = ((bf16[512,8,192]{0,2,1:T(8,128)(2,1)}), bf16[512,8,192]{0,2,1:T(8,128)(2,1)S(1)}, u32[]{:S(2)}, u32[]{:S(2)}) async-start(bf16[512,8,192]{0,2,1:T(8,128)(2,1)} %bitcast.58), calls=%async_computation.1 | async-start | bytes 3145728 | tf_op jit(solution)/shard_map/all_to_all | solution.py:70
  19.2 13.9 %negate_select_fusion.1 = (bf16[512,1,4096]{2,0,1:T(8,128)(2,1)S(1)}, bf16[512,1,4096]{2,0,1:T(8,128)(2,1)}) fusion(bf16[]{:T(256)} %bitcast.14, bf16[]{:T(256)} %bitcast.13, bf16[]{:T(256)} %bitcast.12, bf16[]{:T(256)} %bitcast.11, bf16[]{:T(256)} %bitcast.10, bf16[]{:T(256)} %bitcast.9, bf16[]{:T(256)} %bitcast.8, bf16[]{:T(256)} %bitcast.7, ...), kind=kLoop, calls=%fused_computation.7 | loop fusion | flops 67108864 | bytes 8443920 | tf_op jit(solution)/shard_map/jit(_where)/select_n | solution.py:41
  33.0 6.2 %pad_maximum_fusion = bf16[512,2,4096]{2,0,1:T(8,128)(2,1)} fusion(bf16[512,1,4096]{2,0,1:T(8,128)(2,1)} %get-tuple-element.15, bf16[512,1,4096]{2,0,1:T(8,128)(2,1)S(1)} %get-tuple-element.14), kind=kLoop, calls=%fused_computation | loop fusion | flops 4194304 | bytes 16777216 | tf_op jit(solution)/shard_map/stack | solution.py:42
  39.2 16.4 %copy.36 = bf16[512,2,4096]{2,1,0:T(2,128)(2,1)} copy(bf16[512,2,4096]{2,0,1:T(8,128)(2,1)} %pad_maximum_fusion) | data formatting | bytes 16777216 | tf_op jit(solution)/shard_map/stack | solution.py:42
  55.6 13.1 %reshape.505 = bf16[1024,4096]{1,0:T(8,128)(2,1)} reshape(bf16[512,2,4096]{2,1,0:T(2,128)(2,1)} %copy.36) | data formatting | bytes 16777216 | tf_op jit(solution)/shard_map/reshape | solution.py:73
  68.8 0.0 all-to-all-done.1
  68.8 0.2 copy.50
  68.9 6.3 %convolution_convert_fusion = bf16[1024,192]{0,1:T(8,128)(2,1)S(1)} fusion(bf16[1024,4096]{1,0:T(8,128)(2,1)} %reshape.505, bf16[4096,192]{0,1:T(8,128)(2,1)S(1)} %bitcast.59), kind=kOutput, calls=%fused_computation.15 | convolution fusion | flops 1610809344 | bytes 10354688 | tf_op jit(solution)/shard_map/dot_general | solution.py:74
  75.3 0.2 copy.38
  75.5 0.3 reshape.508
  75.8 1.2 copy.39
  76.9 16.5 %all-to-all-start.2 = ((bf16[256,2,2,2,96]{4,2,3,1,0:T(2,128)(2,1)}), bf16[256,2,2,2,96]{4,2,3,1,0:T(2,128)(2,1)S(1)}, u32[]{:S(2)}, u32[]{:S(2)}) async-start(bf16[256,2,2,2,96]{4,2,3,1,0:T(2,128)(2,1)} %copy.39), calls=%async_computation.2 | async-start | bytes 1048576 | tf_op jit(solution)/shard_map/all_to_all | solution.py:76
  93.4 0.1 fusion.25
  93.5 0.1 copy.48
  93.6 0.3 fusion.22
  94.0 0.3 multiply_subtract_fusion
  94.3 19.2 %all-to-all-done.2 = bf16[256,2,2,2,96]{4,2,3,1,0:T(2,128)(2,1)S(1)} async-done(((bf16[256,2,2,2,96]{4,2,3,1,0:T(2,128)(2,1)}), bf16[256,2,2,2,96]{4,2,3,1,0:T(2,128)(2,1)S(1)}, u32[]{:S(2)}, u32[]{:S(2)}) %all-to-all-start.2) | async-done | bytes 393248 | tf_op jit(solution)/shard_map/all_to_all | solution.py:76
  113.5 1.6 %convolution_bitcast_fusion = f32[2,256,2,192]{1,3,2,0:T(8,128)} fusion(bf16[256,2,2,2,96]{4,2,3,1,0:T(2,128)(2,1)S(1)} %all-to-all-done.2, f32[2,1,96,192]{2,3,1,0:T(8,128)S(1)} %get-tuple-element.10, f32[2,1,96,192]{2,3,1,0:T(8,128)S(1)} %get-tuple-element.9), kind=kOutput, calls=%fused_computation.14 | convolution fusion | flops 453058560 | bytes 1474560 | tf_op jit(solution)/shard_map/sjrfk,jrkc->jsfc/dot_general | solution.py:85
  115.1 1.5 %copy.44 = f32[2,256,2,192]{3,0,2,1:T(2,128)S(1)} copy(f32[2,256,2,192]{1,3,2,0:T(8,128)} %convolution_bitcast_fusion) | data formatting | bytes 1572864 | tf_op jit(solution)/shard_map/sjrfk,jrkc->jsfc/dot_general | solution.py:85
  116.6 2.7 %fusion = f32[2,192,1024]{2,1,0:T(8,128)S(1)} fusion(f32[512,512]{1,0:T(8,128)S(1)} %bitcast.57, f32[512,512]{1,0:T(8,128)S(1)} %bitcast.56, f32[2,512,192]{2,0,1:T(2,128)S(1)} %bitcast.55), kind=kOutput, calls=%fused_computation.11 | convolution fusion | flops 2416443392 | bytes 4456448 | tf_op jit(solution)/shard_map/jts,tw->jsw/dot_general | solution.py:90
  119.4 0.9 fusion.7
  (6 shorter events, 0.2 us)
Async XLA Ops:
  1.3 14.2 %all-to-all-start = ((s32[8,512,3]{1,2,0:T(4,128)}), s32[8,512,3]{1,2,0:T(4,128)S(1)}, u32[]{:S(2)}, u32[]{:S(2)}) async-start(s32[8,512,3]{1,2,0:T(4,128)} %stack.10), calls=%async_computation | async-start | bytes 131072 | tf_op jit(solution)/shard_map/all_to_all | solution.py:13
  15.5 53.2 %all-to-all-start.1 = ((bf16[512,8,192]{0,2,1:T(8,128)(2,1)}), bf16[512,8,192]{0,2,1:T(8,128)(2,1)S(1)}, u32[]{:S(2)}, u32[]{:S(2)}) async-start(bf16[512,8,192]{0,2,1:T(8,128)(2,1)} %bitcast.58), calls=%async_computation.1 | async-start | bytes 3145728 | tf_op jit(solution)/shard_map/all_to_all | solution.py:70
  76.9 36.6 %all-to-all-start.2 = ((bf16[256,2,2,2,96]{4,2,3,1,0:T(2,128)(2,1)}), bf16[256,2,2,2,96]{4,2,3,1,0:T(2,128)(2,1)S(1)}, u32[]{:S(2)}, u32[]{:S(2)}) async-start(bf16[256,2,2,2,96]{4,2,3,1,0:T(2,128)(2,1)} %copy.39), calls=%async_computation.2 | async-start | bytes 1048576 | tf_op jit(solution)/shard_map/all_to_all | solution.py:76
